TPU v7x, 32 devices: a whole 2x2x4 slice. The times are simulated.
32 devices in a mesh: row: 8 (over z, y), col: 4 (over x, core).
Axes of the slice: x: 2, y: 2, z: 4, core: 2. Of those that a mesh axis runs over, the one named last changes fastest.
Arguments:
- tokens: bfloat16 [1024, 4096], P('row'), may hold values from -6 to 6
- in_weight: bfloat16 [4096, 8192], P('row', 'col'), may hold values from -0.09375 to 0.09375
- gate_branch: bfloat16 [1024, 8192], P('row', 'col'), may hold values from -6 to 6
- conv_weight: float32 [4, 8192], P(None, 'col'), may hold values from -3 to 3
- out_weight: bfloat16 [8192, 4096], P('col'), may hold values from -0.0625 to 0.0625
- target: bfloat16 [1024, 4096], P('row'), may hold values from -6 to 6
- lang_ids: int32 [1024], P('row'), may hold values from 0 to 31
- lang_weight: float32 [32], replicated, may hold values from 0.25 to 4
- doc_pos: int32 [1024], P('row'), may hold values from 0 to 127, as said below
Outputs:
- block_out: bfloat16 [1024, 4096], P('row', 'col')
- grad_tokens: bfloat16 [1024, 4096], P('row', 'col')
- grad_gate: bfloat16 [1024, 8192], P('row', 'col')
Inputs may be any that keep to these rules, and one draw needn't show every extreme that they name: doc_pos is 0 at the first token and at every document's first token, and otherwise one more than the previous token's; no document is longer than 128 tokens and one is exactly 128 tokens long; apart from token 0, no document begins within the first 4 tokens of an aligned block of 128 tokens.
All inputs are finite; a program needn't handle non-finite values.
Results may differ from a plain program's by a relative error of at most 0.022.
Values may be sent and summed in bfloat16 or wider, within the bound.
No kernel may reach another device: no remote copies, remote signals or barrier semaphores. Data moves between devices by JAX's collectives and lax.ppermute only.
A program may use at most 128 MiB of HBM per device.

v0:
```python
import jax
import jax.numpy as jnp
from jax import lax
from jax.sharding import PartitionSpec as P

CONV = 4
LANGS = 32


def passed_along(value, axis, steps):
    count = lax.axis_size(axis)
    first, last = (max(0, -steps), min(count, count - steps))
    return lax.ppermute(value, axis, [(source, source + steps) for source in range(first, last)])


def silu_grad(argument):
    sigmoid_v = jax.nn.sigmoid(argument)
    return sigmoid_v * (1.0 + argument * (1.0 - sigmoid_v))


def shards(
    tokens, in_weight, gate_branch, conv_weight, out_weight, target, lang_ids, lang_weight, doc_pos
):
    row_count = tokens.shape[0]
    inner_width = gate_branch.shape[1]
    margin = CONV - 1
    full_in = lax.all_gather(in_weight, "row", axis=0, tiled=True)
    inner_x = jnp.dot(tokens, full_in, preferred_element_type=jnp.float32).astype(jnp.bfloat16)
    from_prev = passed_along(inner_x[row_count - margin :], "row", 1)
    extended = jnp.concatenate([from_prev, inner_x], axis=0).astype(jnp.float32)
    conv_sum = jnp.zeros((row_count, inner_width), jnp.float32)
    for offset in range(CONV):
        keep_mask = (doc_pos >= offset).astype(jnp.float32)[:, None]
        conv_sum = (
            conv_sum
            + conv_weight[offset][None, :]
            * extended[margin - offset : margin - offset + row_count]
            * keep_mask
        )
    gate_value = gate_branch.astype(jnp.float32)
    gate_act = jax.nn.silu(gate_value)
    conv_act = jax.nn.silu(conv_sum)
    mixed = (conv_act * gate_act).astype(jnp.bfloat16)
    partial_value = jnp.dot(mixed, out_weight, preferred_element_type=jnp.float32)
    columns = tokens.shape[1] // lax.axis_size("col")
    col_start = lax.axis_index("col") * columns
    lang_table = (lang_ids[:, None] == jnp.arange(LANGS, dtype=jnp.int32)[None, :]).astype(
        jnp.float32
    )
    token_weight = jnp.sum(lang_table * lang_weight[None, :], axis=1)[:, None]
    out_total = lax.psum(partial_value.astype(jnp.bfloat16), "col").astype(jnp.float32)
    out_block = lax.dynamic_slice_in_dim(out_total, col_start, columns, 1)
    residual_grad = (token_weight * (out_total - target.astype(jnp.float32))).astype(jnp.bfloat16)
    grad_mixed = lax.dot_general(
        residual_grad, out_weight, (((1,), (1,)), ((), ())), preferred_element_type=jnp.float32
    )
    grad_conv = grad_mixed * gate_act * silu_grad(conv_sum)
    grad_gate = (grad_mixed * conv_act * silu_grad(gate_value)).astype(jnp.bfloat16)
    local_grad = conv_weight[0][None, :] * grad_conv
    spill_over = jnp.zeros((margin, inner_width), jnp.float32)
    for offset in range(1, CONV):
        masked = (
            conv_weight[offset][None, :]
            * grad_conv
            * (doc_pos >= offset).astype(jnp.float32)[:, None]
        )
        local_grad = local_grad + jnp.concatenate(
            [masked[offset:], jnp.zeros((offset, inner_width), jnp.float32)], axis=0
        )
        spill_over = spill_over + jnp.concatenate(
            [jnp.zeros((margin - offset, inner_width), jnp.float32), masked[:offset]], axis=0
        )
    from_next = passed_along(spill_over, "row", -1)
    grad_x = (
        local_grad
        + jnp.concatenate(
            [jnp.zeros((row_count - margin, inner_width), jnp.float32), from_next], axis=0
        )
    ).astype(jnp.bfloat16)
    partial_grad = lax.dot_general(
        grad_x, full_in, (((1,), (1,)), ((), ())), preferred_element_type=jnp.float32
    )
    grad_tokens = lax.psum_scatter(
        partial_grad.astype(jnp.bfloat16), "col", scatter_dimension=1, tiled=True
    )
    return (out_block.astype(jnp.bfloat16), grad_tokens, grad_gate)


def solution(mesh):
    in_specs = (
        P("row", None),
        P("row", "col"),
        P("row", "col"),
        P(None, "col"),
        P("col", None),
        P("row", None),
        P("row"),
        P(),
        P("row"),
    )
    out_specs = (P("row", "col"), P("row", "col"), P("row", "col"))
    return jax.shard_map(shards, mesh=mesh, in_specs=in_specs, out_specs=out_specs, check_vma=False)
```

profile of v0, /device:TPU:0, one launch (start us, length us, event | category | flops | bytes accessed | tf_op | source)
XLA Modules:
  0.0 361.6 jit_solution(7084845556274055566)
XLA Ops:
  7.2 0.7 all-gather.2.cloned.1.call-update
  8.0 0.9 fusion.22
  8.9 231.6 %all-gather.2.cloned.1.call-done = bf16[4096,2048]{1,0:T(8,128)(2,1)} async-done(((bf16[512,2048]{1,0:T(8,128)(2,1)}), bf16[4096,2048]{1,0:T(8,128)(2,1)}) %all-gather.2.cloned.1.call-update) | async-done | bytes 16777232 | tf_op jit(solution)/shard_map/all_gather | solution.py:27
  240.5 8.3 %convolution_convert_fusion.2 = bf16[128,2048]{1,0:T(8,128)(2,1)S(1)} fusion(bf16[128,4096]{1,0:T(8,128)(2,1)S(1)} %copy-done, bf16[4096,2048]{1,0:T(8,128)(2,1)} %all-gather.2.cloned.1.call-done), kind=kOutput, calls=%fused_computation.2 | convolution fusion | flops 2147745792 | bytes 18350080 | tf_op jit(solution)/shard_map/dot_general | solution.py:28
  248.8 2.7 collective-permute-start
  251.5 1.4 collective-permute-done
  252.9 0.1 maximum_convert_fusion
  253.1 0.7 fusion.9
  253.8 1.0 copy-done.2
  254.8 3.8 %convolution_convert_fusion.1 = bf16[128,4096]{1,0:T(8,128)(2,1)} fusion(bf16[2048,4096]{1,0:T(8,128)(2,1)S(1)} %copy-done.4, bf16[128,2048]{1,0:T(8,128)(2,1)S(1)} %copy-done.5, f32[128,2048]{1,0:T(8,128)S(1)} %fusion.9), kind=kOutput, calls=%fused_computation.1 | convolution fusion | flops 2150891520 | bytes 19398656 | tf_op jit(solution)/shard_map/dot_general | solution.py:44
  258.6 0.0 reduce-scatter.2.cloned.1.call-start
  258.7 0.1 select_reduce_fusion
  258.8 36.9 %all-reduce.8.cloned.1.call-done = bf16[128,4096]{1,0:T(8,128)(2,1)} async-done(((bf16[128,4096]{1,0:T(8,128)(2,1)}), bf16[128,4096]{1,0:T(8,128)(2,1)}) %all-reduce.8.cloned.1.call-update) | async-done | bytes 1048592 | tf_op jit(solution)/shard_map/psum | solution.py:51
  295.7 13.7 %multiply_multiply_fusion.2 = (f32[128,2048]{1,0:T(8,128)S(1)}, f32[128,2048]{1,0:T(8,128)S(1)}, bf16[128,2048]{1,0:T(8,128)(2,1)}) fusion(f32[128]{0:T(128)S(1)} %get-tuple-element.13, f32[2048]{0:T(1024)S(1)} %bitcast.16, f32[128,2048]{1,0:T(8,128)} %copy-done.2, bf16[128,2048]{1,0:T(8,128)(2,1)} %param.11, bf16[2048,4096]{1,0:T(8,128)(2,1)} %param.13, ...), kind=kOutput, calls=%fused_computation.29 | convolution fusion | flops 2156396544 | bytes 23077888 | tf_op jit(solution)/shard_map/dot_general | solution.py:54
  309.4 0.3 multiply_multiply_fusion.1
  309.8 0.7 copy-done.1
  310.4 1.5 collective-permute-start.1
  311.9 1.3 slice.69
  313.2 1.1 slice.70
  314.3 1.1 slice.71
  315.4 0.8 collective-permute-done.1
  316.2 13.1 %convolution_convert_fusion = bf16[128,4096]{1,0:T(8,128)(2,1)} fusion(bf16[4096,2048]{1,0:T(8,128)(2,1)} %all-gather.2.cloned.1.call-done, f32[3,2048]{1,0:T(4,128)S(1)} %collective-permute-done.1, f32[125,2048]{1,0:T(8,128)} %slice.71, f32[126,2048]{1,0:T(8,128)} %slice.70, f32[127,2048]{1,0:T(8,128)S(1)} %slice.69, f32[128,2048]{1,0:T(8,128)S(1)} %get-tuple-element.4, ...), kind=kOutput, calls=%fused_computation | convolution fusion | flops 2149580800 | bytes 22003712 | tf_op jit(solution)/shard_map/dot_general | solution.py:80
  329.3 1.7 dynamic-slice_convert_fusion
  331.0 24.1 %reduce-scatter.2.cloned.1.call-done = bf16[128,1024]{1,0:T(8,128)(2,1)} async-done(((bf16[128,4096]{1,0:T(8,128)(2,1)}), bf16[128,1024]{1,0:T(8,128)(2,1)}) %reduce-scatter.2.cloned.1.call-update) | async-done | bytes 262160 | tf_op jit(solution)/shard_map/reduce_scatter | solution.py:83
  (23 shorter events, 0.2 us)
Async XLA Ops:
  7.2 233.3 %copy-start = (bf16[128,4096]{1,0:T(8,128)(2,1)S(1)}, bf16[128,4096]{1,0:T(8,128)(2,1)}, u32[]{:S(2)}) copy-start(bf16[128,4096]{1,0:T(8,128)(2,1)} %param.9) | copy-start | bytes 3145732
  7.2 244.3 %copy-start.3 = (s32[128]{0:T(128)S(1)}, s32[128]{0:T(128)}, u32[]{:S(2)}) copy-start(s32[128]{0:T(128)} %param.17) | copy-start | bytes 1540
  7.2 247.6 %copy-start.5 = (bf16[128,2048]{1,0:T(8,128)(2,1)S(1)}, bf16[128,2048]{1,0:T(8,128)(2,1)}, u32[]{:S(2)}) copy-start(bf16[128,2048]{1,0:T(8,128)(2,1)} %param.11) | copy-start | bytes 1572868
  7.2 233.3 %all-gather.2.cloned.1.call-start = ((), (), s32[]{:S(2)}) async-start(), calls=%async_computation.1 | async-start | bytes 18874368 | tf_op jit(solution)/shard_map/all_gather | solution.py:27
  7.9 287.8 %all-reduce.8.cloned.1.call-start = ((), (), s32[]{:S(2)}) async-start(), calls=%async_computation.2 | async-start | bytes 2097152 | tf_op jit(solution)/shard_map/psum | solution.py:51
  240.5 14.3 %copy-start.4 = (bf16[2048,4096]{1,0:T(8,128)(2,1)S(1)}, bf16[2048,4096]{1,0:T(8,128)(2,1)}, u32[]{:S(2)}) copy-start(bf16[2048,4096]{1,0:T(8,128)(2,1)} %param.13) | copy-start | bytes 50331652
  248.8 4.2 %collective-permute-start = (bf16[3,2048]{1,0:T(4,128)(2,1)S(1)}, bf16[3,2048]{1,0:T(4,128)(2,1)S(1)}, u32[]{:S(2)}, u32[]{:S(2)}) collective-permute-start(bf16[3,2048]{1,0:T(4,128)(2,1)S(1)} %slice.64), channel_id=1, source_target_pairs={{0,4},{4,8},{8,12},{12,16},{16,20},{20,24},{24,28},{1,5},{5,9},{9,... | collective-permute-start | bytes 36872 | tf_op jit(solution)/shard_map/ppermute | solution.py:13
  253.8 1.0 copy-start.2
  254.8 3.8 %copy-start.6 = (f32[32]{0:T(128)S(1)}, f32[32]{0:T(128)}, u32[]{:S(2)}) copy-start(f32[32]{0:T(128)} %param.16) | copy-start | bytes 388
  254.8 3.9 %copy-start.7 = (s32[128]{0:T(128)S(1)}, s32[128]{0:T(128)}, u32[]{:S(2)}) copy-start(s32[128]{0:T(128)} %param.15) | copy-start | bytes 1540
  258.6 96.5 %reduce-scatter.2.cloned.1.call-start = ((), (), s32[]{:S(2)}) async-start(), calls=%async_computation.3 | async-start | bytes 1310720 | tf_op jit(solution)/shard_map/reduce_scatter | solution.py:83
  309.4 1.0 copy-start.1
  310.4 5.8 %collective-permute-start.1 = (f32[3,2048]{1,0:T(4,128)S(1)}, f32[3,2048]{1,0:T(4,128)S(1)}, u32[]{:S(2)}, u32[]{:S(2)}) collective-permute-start(f32[3,2048]{1,0:T(4,128)S(1)} %slice_add_fusion), channel_id=1, source_target_pairs={{4,0},{8,4},{12,8},{16,12},{20,16},{24,20},{28,24},{5,1},{9,5},{13... | collective-permute-start | bytes 73736 | tf_op jit(solution)/shard_map/ppermute | solution.py:13
Sparse Core Ops, SparseCore 0:
  10.2 230.2 all-gather.1
  258.8 36.9 all-reduce.7
  329.4 25.6 reduce-scatter.1
where the time goes:
time: 362 us
  waiting for transfers between devices  296 us (82%)
  matrix products  38.8 us (11%)
  between operations  13.9 us (4%)
  local copies, waits for them, and re-layouts  7.83 us (2%)
  starting transfers between devices  4.3 us (1%)
    all_gather x1, waiting for transfers between devices, shards(): full_in = lax.all_gather(in_weight, 'row', axis=0, tiled=True)  232 us
    psum x1, waiting for transfers between devices, shards(): lax.psum(partial_value.astype(jnp.bfloat16), 'col').astype(jnp.float32)  36.9 us
    reduce_scatter x1, waiting for transfers between devices, shards(): lax.psum_scatter(partial_grad.astype(jnp.bfloat16), 'col', scatter_dimens...  24.1 us
    dot_general x1, matrix products, shards(): lax.dot_general(residual_grad, out_weight, (((1,), (1,)), ((), ())), pref...  13.7 us
    dot_general x1, matrix products, shards(): lax.dot_general(grad_x, full_in, (((1,), (1,)), ((), ())), preferred_elem...  13.1 us
    dot_general x1, matrix products, shards(): jnp.dot(tokens, full_in, preferred_element_type=jnp.float32)  8.25 us
  transfers between devices with their start and end apart: 5, of which 5 were waited for; matrix products, arithmetic and copies ran while one was open for 2% of the time, Pallas kernels for 0%

commit v1 on v0

--- a/solution.py
+++ b/solution.py
@@ -5,6 +5,12 @@
 
 CONV = 4
 LANGS = 32
+
+
+def laid_out(blocks, dim):
+    blocks = jnp.moveaxis(blocks, 0, dim)
+    dims = blocks.shape
+    return blocks.reshape(*dims[:dim], dims[dim] * dims[dim + 1], *dims[dim + 2 :])
 
 
 def passed_along(value, axis, steps):
@@ -24,7 +30,19 @@
     row_count = tokens.shape[0]
     inner_width = gate_branch.shape[1]
     margin = CONV - 1
-    full_in = lax.all_gather(in_weight, "row", axis=0, tiled=True)
+    length = lax.axis_size("row")
+    pairs = [(i, (i + 1) % length) for i in range(length)]
+    back = [(b, a) for a, b in pairs]
+    lower, upper = ([], [])
+    for step in range(length - 1):
+        if step % 2 == 0:
+            lower.append(lax.ppermute(lower[-1] if lower else in_weight, "row", pairs))
+        else:
+            upper.append(lax.ppermute(upper[-1] if upper else in_weight, "row", back))
+    pieces = jnp.stack([*lower[::-1], in_weight, *upper])
+    shift = lax.axis_index("row") - len(lower)
+    pieces = pieces[(jnp.arange(length) - shift) % length]
+    full_in = laid_out(pieces, 0)
     inner_x = jnp.dot(tokens, full_in, preferred_element_type=jnp.float32).astype(jnp.bfloat16)
     from_prev = passed_along(inner_x[row_count - margin :], "row", 1)
     extended = jnp.concatenate([from_prev, inner_x], axis=0).astype(jnp.float32)

time: 362 us -> 503 us (1.39)
  waiting for transfers between devices: 296 us -> 367 us
  local copies, waits for them, and re-layouts: 7.83 us -> 50 us
  starting transfers between devices: 4.3 us -> 23.2 us
  other arithmetic: 1.27 us -> 9.09 us
    ppermute x0 -> x7, waiting for transfers between devices: none -> 306 us  [the longest x4 306 us: shards(): lower.append(lax.ppermute(lower[-1] if lower else in_weight, 'row', pairs))]
    all_gather x1 -> x0, waiting for transfers between devices: 232 us -> none  [shards(): full_in = lax.all_gather(in_weight, 'row', axis=0, tiled=True)]
    gather x0 -> x3, local copies, waits for them, and re-layouts: none -> 22.6 us  [shards(): pieces = pieces[(jnp.arange(length) - shift) % length]]
    unnamed x16 -> x29, local copies, waits for them, and re-layouts: 1.69 us -> 21.2 us
    ppermute x0 -> x7, starting transfers between devices: none -> 17.2 us  [the longest x3 9.15 us: shards(): upper.append(lax.ppermute(upper[-1] if upper else in_weight, 'row', back))]
    unnamed x0 -> x1, other arithmetic: none -> 7.8 us
    dot_general x1, matrix products: 8.25 us -> 2.52 us  [shards(): jnp.dot(tokens, full_in, preferred_element_type=jnp.float32)]
    dot_general x1, matrix products: 3.76 us -> 9.46 us  [shards(): jnp.dot(mixed, out_weight, preferred_element_type=jnp.float32)]
  transfers between devices with their start and end apart: 5 -> 11, of which waited for: 5 -> 8; matrix products, arithmetic and copies ran while one was open for 2% -> 3% of each run, Pallas kernels for 0% -> 0%
where the time goes in v1:
time: 503 us; the launch traced here: 502 us
  waiting for transfers between devices  367 us (73%)
  local copies, waits for them, and re-layouts  50 us (10%)
  matrix products  38.7 us (8%)
  starting transfers between devices  23.2 us (5%)
  between operations  14.3 us (3%)
  other arithmetic  9.09 us (2%)
    ppermute x4, waiting for transfers between devices, shards(): lower.append(lax.ppermute(lower[-1] if lower else in_weight, 'row', pairs))  306 us
    psum x1, waiting for transfers between devices, shards(): lax.psum(partial_value.astype(jnp.bfloat16), 'col').astype(jnp.float32)  34.6 us
    reduce_scatter x1, waiting for transfers between devices, shards(): lax.psum_scatter(partial_grad.astype(jnp.bfloat16), 'col', scatter_dimens...  23.9 us
    gather x3, local copies, waits for them, and re-layouts, shards(): pieces = pieces[(jnp.arange(length) - shift) % length]  22.6 us
    unnamed x29, local copies, waits for them, and re-layouts  21.2 us
    dot_general x1, matrix products, shards(): lax.dot_general(residual_grad, out_weight, (((1,), (1,)), ((), ())), pref...  13.7 us
    dot_general x1, matrix products, shards(): lax.dot_general(grad_x, full_in, (((1,), (1,)), ((), ())), preferred_elem...  13.1 us
  transfers between devices with their start and end apart: 11, of which 8 were waited for; matrix products, arithmetic and copies ran while one was open for 3% of the time, Pallas kernels for 0%

profile of v1, /device:TPU:0, one launch (start us, length us, event | category | flops | bytes accessed | tf_op | source)
XLA Modules:
  0.0 502.4 jit_solution(760550495808361924)
XLA Ops:
  7.2 3.0 collective-permute-start
  10.3 48.9 %collective-permute-done = bf16[512,2048]{1,0:T(8,128)(2,1)S(1)} collective-permute-done((bf16[512,2048]{1,0:T(8,128)(2,1)}, bf16[512,2048]{1,0:T(8,128)(2,1)S(1)}, u32[]{:S(2)}, u32[]{:S(2)}) %collective-permute-start) | collective-permute-done | bytes 2097184 | tf_op jit(solution)/shard_map/ppermute | solution.py:39
  60.5 4.7 collective-permute-start.4
  65.2 84.8 %collective-permute-done.1 = bf16[512,2048]{1,0:T(8,128)(2,1)S(1)} collective-permute-done((bf16[512,2048]{1,0:T(8,128)(2,1)S(1)}, bf16[512,2048]{1,0:T(8,128)(2,1)S(1)}, u32[]{:S(2)}, u32[]{:S(2)}) %collective-permute-start.1) | collective-permute-done | bytes 2097184 | tf_op jit(solution)/shard_map/ppermute | solution.py:39
  151.4 2.5 collective-permute-start.2
  153.9 2.2 collective-permute-start.5
  156.1 86.4 %collective-permute-done.2 = bf16[512,2048]{1,0:T(8,128)(2,1)} collective-permute-done((bf16[512,2048]{1,0:T(8,128)(2,1)S(1)}, bf16[512,2048]{1,0:T(8,128)(2,1)}, u32[]{:S(2)}, u32[]{:S(2)}) %collective-permute-start.2) | collective-permute-done | bytes 2097184 | tf_op jit(solution)/shard_map/ppermute | solution.py:39
  242.5 2.6 collective-permute-start.3
  246.1 2.2 collective-permute-start.6
  248.3 86.0 %collective-permute-done.3 = bf16[512,2048]{1,0:T(8,128)(2,1)} collective-permute-done((bf16[512,2048]{1,0:T(8,128)(2,1)}, bf16[512,2048]{1,0:T(8,128)(2,1)}, u32[]{:S(2)}, u32[]{:S(2)}) %collective-permute-start.3) | collective-permute-done | bytes 2097184 | tf_op jit(solution)/shard_map/ppermute | solution.py:39
  339.8 1.8 bitcast_dynamic-update-slice_fusion.4
  345.6 6.5 %fusion.25 = (bf16[8,512,1024]{2,1,0:T(8,128)(2,1)}, bf16[8,512,1024]{2,1,0:T(8,128)(2,1)}) fusion(bf16[8,512,2048]{2,1,0:T(8,128)(2,1)S(1)} %bitcast_dynamic-update-slice_fusion), kind=kLoop, calls=%fused_computation.67 | loop fusion | bytes 33554432 | tf_op jit(solution)/shard_map/gather | solution.py:44
  352.1 8.1 %gather_fusion = bf16[8,512,1024]{2,1,0:T(8,128)(2,1)} fusion(bf16[8,512,1024]{2,1,0:T(8,128)(2,1)} %get-tuple-element.5, s32[1024]{0:T(1024)S(1)} %pad_clamp_fusion), kind=kCustom, calls=%fused_computation | custom fusion | bytes 16777248 | tf_op jit(solution)/shard_map/gather | solution.py:44
  360.1 8.1 %gather_fusion.1 = bf16[8,512,1024]{2,1,0:T(8,128)(2,1)} fusion(bf16[8,512,1024]{2,1,0:T(8,128)(2,1)} %get-tuple-element.6, s32[1024]{0:T(1024)S(1)} %pad_clamp_fusion), kind=kCustom, calls=%fused_computation.1 | custom fusion | bytes 16777248 | tf_op jit(solution)/shard_map/gather | solution.py:44
  368.2 7.8 %pad_maximum_fusion = bf16[8,512,2048]{2,1,0:T(8,128)(2,1)S(1)} fusion(bf16[8,512,1024]{2,1,0:T(8,128)(2,1)} %gather_fusion.1, bf16[8,512,1024]{2,1,0:T(8,128)(2,1)} %gather_fusion), kind=kLoop, calls=%fused_computation.2 | loop fusion | flops 33554432 | bytes 33554432
  376.1 5.7 %copy-done.1 = bf16[8,512,2048]{2,1,0:T(8,128)(2,1)} copy-done((bf16[8,512,2048]{2,1,0:T(8,128)(2,1)}, bf16[8,512,2048]{2,1,0:T(8,128)(2,1)S(1)}, u32[]{:S(2)}) %copy-start.1) | copy-done | bytes 16777240
  381.8 2.5 fusion
  384.3 4.4 collective-permute-start.7
  392.0 9.5 %convolution_convert_fusion.1 = bf16[128,4096]{1,0:T(8,128)(2,1)} fusion(bf16[2048,4096]{1,0:T(8,128)(2,1)} %param.13, bf16[128,2048]{1,0:T(8,128)(2,1)S(1)} %copy-done.8, f32[128,2048]{1,0:T(8,128)S(1)} %fusion.10), kind=kOutput, calls=%fused_computation.4 | convolution fusion | flops 2150891520 | bytes 19398656 | tf_op jit(solution)/shard_map/dot_general | solution.py:62
  401.8 34.6 %all-reduce.8.cloned.1.call-done = bf16[128,4096]{1,0:T(8,128)(2,1)} async-done(((bf16[128,4096]{1,0:T(8,128)(2,1)}), bf16[128,4096]{1,0:T(8,128)(2,1)}) %all-reduce.8.cloned.1.call-update) | async-done | bytes 1048592 | tf_op jit(solution)/shard_map/psum | solution.py:69
  436.4 13.7 %multiply_multiply_fusion.2 = (f32[128,2048]{1,0:T(8,128)S(1)}, f32[128,2048]{1,0:T(8,128)S(1)}, bf16[128,2048]{1,0:T(8,128)(2,1)}) fusion(f32[128]{0:T(128)S(1)} %get-tuple-element.15, f32[2048]{0:T(1024)S(1)} %bitcast.39, f32[128,2048]{1,0:T(8,128)} %copy-done.6, bf16[128,2048]{1,0:T(8,128)(2,1)} %param.11, bf16[2048,4096]{1,0:T(8,128)(2,1)} %param.13, ...), kind=kOutput, calls=%fused_computation.41 | convolution fusion | flops 2156396544 | bytes 23077888 | tf_op jit(solution)/shard_map/dot_general | solution.py:72
  453.6 2.3 slice.73
  456.9 13.1 %convolution_convert_fusion = bf16[128,4096]{1,0:T(8,128)(2,1)} fusion(bf16[4096,2048]{1,0:T(8,128)(2,1)} %bitcast.31, f32[3,2048]{1,0:T(4,128)S(1)} %collective-permute-done.8, f32[125,2048]{1,0:T(8,128)} %slice.75, f32[126,2048]{1,0:T(8,128)S(1)} %slice.74, f32[127,2048]{1,0:T(8,128)} %slice.73, f32[128,2048]{1,0:T(8,128)S(1)} %get-tuple-element.4, ...), kind=kOutput, calls=%fused_computation.3 | convolution fusion | flops 2149580800 | bytes 22003712 | tf_op jit(solution)/shard_map/dot_general | solution.py:98
  471.7 23.9 %reduce-scatter.2.cloned.1.call-done = bf16[128,1024]{1,0:T(8,128)(2,1)} async-done(((bf16[128,4096]{1,0:T(8,128)(2,1)}), bf16[128,1024]{1,0:T(8,128)(2,1)}) %reduce-scatter.2.cloned.1.call-update) | async-done | bytes 262160 | tf_op jit(solution)/shard_map/reduce_scatter | solution.py:101
  (54 shorter events, 22.8 us)
Async XLA Ops:
  7.2 374.6 %copy-start = (bf16[128,4096]{1,0:T(8,128)(2,1)S(1)}, bf16[128,4096]{1,0:T(8,128)(2,1)}, u32[]{:S(2)}) copy-start(bf16[128,4096]{1,0:T(8,128)(2,1)} %param.9) | copy-start | bytes 3145732
  7.2 334.4 %copy-start.2 = (bf16[512,2048]{1,0:T(8,128)(2,1)S(1)}, bf16[512,2048]{1,0:T(8,128)(2,1)}, u32[]{:S(2)}) copy-start(bf16[512,2048]{1,0:T(8,128)(2,1)} %param.10) | copy-start | bytes 6291460
  7.2 429.2 %all-reduce.8.cloned.1.call-start = ((), (), s32[]{:S(2)}) async-start(), calls=%async_computation.1 | async-start | bytes 2097152 | tf_op jit(solution)/shard_map/psum | solution.py:69
  7.2 51.9 %collective-permute-start = (bf16[512,2048]{1,0:T(8,128)(2,1)}, bf16[512,2048]{1,0:T(8,128)(2,1)S(1)}, u32[]{:S(2)}, u32[]{:S(2)}) collective-permute-start(bf16[512,2048]{1,0:T(8,128)(2,1)} %param.10), channel_id=1, source_target_pairs={{0,4},{4,8},{8,12},{12,16},{16,20},{20,24},{24,28},{28,0},{1,5},{5... | collective-permute-start | bytes 6291464 | tf_op jit(solution)/shard_map/ppermute | solution.py:39
  59.1 1.3 copy-start.3
  60.5 89.6 %collective-permute-start.1 = (bf16[512,2048]{1,0:T(8,128)(2,1)S(1)}, bf16[512,2048]{1,0:T(8,128)(2,1)S(1)}, u32[]{:S(2)}, u32[]{:S(2)}) collective-permute-start(bf16[512,2048]{1,0:T(8,128)(2,1)S(1)} %collective-permute-done), channel_id=1, source_target_pairs={{0,4},{4,8},{8,12},{12,16},{16,20},{20,24},{24,28},{28,0},{1,5},{5... | collective-permute-start | bytes 6291464 | tf_op jit(solution)/shard_map/ppermute | solution.py:39
  60.5 93.4 %collective-permute-start.4 = (bf16[512,2048]{1,0:T(8,128)(2,1)}, bf16[512,2048]{1,0:T(8,128)(2,1)}, u32[]{:S(2)}, u32[]{:S(2)}) collective-permute-start(bf16[512,2048]{1,0:T(8,128)(2,1)} %param.10), channel_id=1, source_target_pairs={{4,0},{8,4},{12,8},{16,12},{20,16},{24,20},{28,24},{0,28},{5,1},{9... | collective-permute-start | bytes 6291464 | tf_op jit(solution)/shard_map/ppermute | solution.py:41
  150.0 1.4 copy-start.4
  151.4 91.1 %collective-permute-start.2 = (bf16[512,2048]{1,0:T(8,128)(2,1)S(1)}, bf16[512,2048]{1,0:T(8,128)(2,1)}, u32[]{:S(2)}, u32[]{:S(2)}) collective-permute-start(bf16[512,2048]{1,0:T(8,128)(2,1)S(1)} %collective-permute-done.1), channel_id=1, source_target_pairs={{0,4},{4,8},{8,12},{12,16},{16,20},{20,24},{24,28},{28,0},{1,5},{5... | collective-permute-start | bytes 6291464 | tf_op jit(solution)/shard_map/ppermute | solution.py:39
  153.9 92.2 %collective-permute-start.5 = (bf16[512,2048]{1,0:T(8,128)(2,1)}, bf16[512,2048]{1,0:T(8,128)(2,1)}, u32[]{:S(2)}, u32[]{:S(2)}) collective-permute-start(bf16[512,2048]{1,0:T(8,128)(2,1)} %collective-permute-done.4), channel_id=1, source_target_pairs={{4,0},{8,4},{12,8},{16,12},{20,16},{24,20},{28,24},{0,28},{5,1},{9... | collective-permute-start | bytes 6291464 | tf_op jit(solution)/shard_map/ppermute | solution.py:41
  242.5 91.7 %collective-permute-start.3 = (bf16[512,2048]{1,0:T(8,128)(2,1)}, bf16[512,2048]{1,0:T(8,128)(2,1)}, u32[]{:S(2)}, u32[]{:S(2)}) collective-permute-start(bf16[512,2048]{1,0:T(8,128)(2,1)} %collective-permute-done.2), channel_id=1, source_target_pairs={{0,4},{4,8},{8,12},{12,16},{16,20},{20,24},{24,28},{28,0},{1,5},{5... | collective-permute-start | bytes 6291464 | tf_op jit(solution)/shard_map/ppermute | solution.py:39
  246.1 99.4 %collective-permute-start.6 = (bf16[512,2048]{1,0:T(8,128)(2,1)}, bf16[512,2048]{1,0:T(8,128)(2,1)S(1)}, u32[]{:S(2)}, u32[]{:S(2)}) collective-permute-start(bf16[512,2048]{1,0:T(8,128)(2,1)} %collective-permute-done.5), channel_id=1, source_target_pairs={{4,0},{8,4},{12,8},{16,12},{20,16},{24,20},{28,24},{0,28},{5,1},{9... | collective-permute-start | bytes 6291464 | tf_op jit(solution)/shard_map/ppermute | solution.py:41
  376.0 5.7 %copy-start.1 = (bf16[8,512,2048]{2,1,0:T(8,128)(2,1)}, bf16[8,512,2048]{2,1,0:T(8,128)(2,1)S(1)}, u32[]{:S(2)}) copy-start(bf16[8,512,2048]{2,1,0:T(8,128)(2,1)S(1)} %pad_maximum_fusion) | copy-start | bytes 50331652
  376.1 12.7 %copy-start.7 = (s32[128]{0:T(128)S(1)}, s32[128]{0:T(128)}, u32[]{:S(2)}) copy-start(s32[128]{0:T(128)} %param.17) | copy-start | bytes 1540
  376.1 15.9 %copy-start.8 = (bf16[128,2048]{1,0:T(8,128)(2,1)S(1)}, bf16[128,2048]{1,0:T(8,128)(2,1)}, u32[]{:S(2)}) copy-start(bf16[128,2048]{1,0:T(8,128)(2,1)} %param.11) | copy-start | bytes 1572868
  384.3 5.8 %collective-permute-start.7 = (bf16[3,2048]{1,0:T(4,128)(2,1)S(1)}, bf16[3,2048]{1,0:T(4,128)(2,1)S(1)}, u32[]{:S(2)}, u32[]{:S(2)}) collective-permute-start(bf16[3,2048]{1,0:T(4,128)(2,1)S(1)} %slice.68), channel_id=1, source_target_pairs={{0,4},{4,8},{8,12},{12,16},{16,20},{20,24},{24,28},{1,5},{5,9},{9,... | collective-permute-start | bytes 36872 | tf_op jit(solution)/shard_map/ppermute | solution.py:19
  391.1 1.0 copy-start.6
  392.0 9.7 %copy-start.9 = (f32[32]{0:T(128)S(1)}, f32[32]{0:T(128)}, u32[]{:S(2)}) copy-start(f32[32]{0:T(128)} %param.16) | copy-start | bytes 388
  392.0 9.7 %copy-start.10 = (s32[128]{0:T(128)S(1)}, s32[128]{0:T(128)}, u32[]{:S(2)}) copy-start(s32[128]{0:T(128)} %param.15) | copy-start | bytes 1540
  401.5 94.0 %reduce-scatter.2.cloned.1.call-start = ((), (), s32[]{:S(2)}) async-start(), calls=%async_computation.2 | async-start | bytes 1310720 | tf_op jit(solution)/shard_map/reduce_scatter | solution.py:101
  450.1 1.0 copy-start.5
  451.1 5.8 %collective-permute-start.8 = (f32[3,2048]{1,0:T(4,128)S(1)}, f32[3,2048]{1,0:T(4,128)S(1)}, u32[]{:S(2)}, u32[]{:S(2)}) collective-permute-start(f32[3,2048]{1,0:T(4,128)S(1)} %slice_add_fusion), channel_id=1, source_target_pairs={{4,0},{8,4},{12,8},{16,12},{20,16},{24,20},{28,24},{5,1},{9,5},{13... | collective-permute-start | bytes 73736 | tf_op jit(solution)/shard_map/ppermute | solution.py:19
Sparse Core Ops, SparseCore 0:
  401.6 34.7 all-reduce.7
  470.1 25.3 reduce-scatter.1
